TPU v7x, 128 devices: a whole 4x4x4 slice. The times are simulated.
128 devices in a mesh: dp: 16 (over x, y), feat: 8 (over z, core).
Axes of the slice: x: 4, y: 4, z: 4, core: 2. Of those that a mesh axis runs over, the one named last changes fastest.
Arguments:
- images: bfloat16 [8192, 3072], P(('dp', 'feat')), may hold values from -6 to 6
- labels: int32 [8192], P('dp'), may hold values from 0 to 999
- predictions: float32 [8192, 1000], P('dp'), may hold values from -2 to 2
- filters: bfloat16 [75, 1024], P(None, 'feat'), may hold values from -0.75 to 0.75
- biases: float32 [1024], P('feat'), may hold values from -3 to 3
Outputs:
- weights: float32 [4096, 1000], P('feat')
- new_residual: float32 [8192, 1000], P(('dp', 'feat'))
All inputs are finite; a program needn't handle non-finite values.
Results may differ from a plain program's by a relative error of at most 0.007.
The roundings to bfloat16 on the way count: a program that leaves them out, or rounds other values in their place, can miss the bound.
Values may be sent and summed in bfloat16 or wider, within the bound.
No kernel may reach another device: no remote copies, remote signals or barrier semaphores. Data moves between devices by JAX's collectives and lax.ppermute only.
A program may use at most 192 MiB of HBM per device.

v0:
```python
import math
import jax
import jax.numpy as jnp
from jax import lax
from jax.sharding import PartitionSpec as P

SIDE = 32
CHAN = 3
KSIZE = 5


def chol_solve(factor, rhs):
    middle = lax.linalg.triangular_solve(factor, rhs, left_side=True, lower=True, transpose_a=False)
    return lax.linalg.triangular_solve(factor, middle, left_side=True, lower=True, transpose_a=True)


def split_parts(values):
    upper = values.astype(jnp.bfloat16)
    lower = (values - upper.astype(jnp.float32)).astype(jnp.bfloat16)
    return (upper, lower)


def left_product(feats, other):
    return lax.dot_general(
        feats, other, (((0,), (0,)), ((), ())), preferred_element_type=jnp.float32
    )


def conv_pool(imgs, kernel, offsets):
    count = imgs.shape[0]
    filt_count = kernel.shape[3]
    pics = imgs.reshape(count, SIDE, SIDE, CHAN)
    response = lax.conv_general_dilated(
        pics,
        kernel,
        (1, 1),
        "VALID",
        dimension_numbers=("NHWC", "HWIO", "NHWC"),
        preferred_element_type=jnp.float32,
    )
    response = jnp.maximum(response + offsets, 0.0)
    half = (SIDE - KSIZE + 1) // 2
    pooled = response.reshape(count, 2, half, 2, half, filt_count).mean(axis=(2, 4))
    return jnp.transpose(pooled, (0, 3, 1, 2)).reshape(count, 4 * filt_count).astype(jnp.bfloat16)


def shards(images, labels, predictions, filters, biases):
    filt_count = filters.shape[1]
    kernel = filters.reshape(KSIZE, KSIZE, CHAN, filt_count)
    share = images.shape[0]
    total_images = share * lax.axis_size("feat") * lax.axis_size("dp")
    piece = lax.all_gather(images, "feat", axis=0, tiled=True)
    count = piece.shape[0]
    group = math.gcd(count, 128)
    blocks = piece.reshape(count // group, group, piece.shape[1])
    out = lax.map(lambda part: conv_pool(part, kernel, biases), blocks)
    feats = out.reshape(count, 4 * filt_count)
    width = feats.shape[1]
    residual = (
        labels[:, None] == jnp.arange(predictions.shape[1], dtype=jnp.int32)[None, :]
    ).astype(jnp.float32) - predictions
    res_upper, res_lower = split_parts(residual)
    gram = lax.psum(left_product(feats, feats), "dp")
    cross = left_product(feats, res_upper) + left_product(feats, res_lower)
    cross, gram = lax.optimization_barrier((cross, gram))
    cross = lax.psum(cross, "dp")
    gram = gram / total_images + 0.5 * jnp.eye(width, dtype=jnp.float32)
    cross = cross / total_images
    factor = jnp.linalg.cholesky(gram)
    solved = chol_solve(factor, cross)
    sol_upper, sol_lower = split_parts(solved)
    fitted = lax.psum_scatter(
        (
            jnp.dot(feats, sol_upper, preferred_element_type=jnp.float32)
            + jnp.dot(feats, sol_lower, preferred_element_type=jnp.float32)
        ).astype(jnp.bfloat16),
        "feat",
        scatter_dimension=0,
        tiled=True,
    ).astype(jnp.float32)
    mine = lax.dynamic_slice_in_dim(residual, lax.axis_index("feat") * share, share, 0)
    return (solved, mine - fitted)


def solution(mesh):
    placed = (P(("dp", "feat"), None), P("dp"), P("dp", None), P(None, "feat"), P("feat"))
    return jax.shard_map(
        shards,
        mesh=mesh,
        in_specs=placed,
        out_specs=(P("feat", None), P(("dp", "feat"), None)),
        check_vma=False,
    )
```

profile of v0, /device:TPU:0, one launch (start us, length us, event | category | flops | bytes accessed | tf_op | source)
XLA Modules:
  0.0 528.2 jit_solution(10686514619989856401)
XLA Ops:
  8.7 2.9 copy.22
  12.1 28.0 %all-gather.2.cloned.1.call-done = bf16[512,3072]{1,0:T(8,128)(2,1)} async-done(((bf16[64,3072]{1,0:T(8,128)(2,1)}), bf16[512,3072]{1,0:T(8,128)(2,1)}) %all-gather.2.cloned.1.call-update) | async-done | bytes 3145744 | tf_op jit(solution)/shard_map/all_gather | solution.py:52
  40.1 152.3 %while.11 = (s32[]{:T(128)}, bf16[4,128,512]{1,2,0:T(8,128)(2,1)}, bf16[4,128,3072]{2,1,0:T(8,128)(2,1)}, bf16[5,5,3,128]{3,2,1,0:T(4,128)(2,1)S(1)}, f32[128]{0:T(128)S(1)}, /*index=5*/s32[]{:T(128)}, f32[]{:T(128)}) while((s32[]{:T(128)}, bf16[4,128,512]{1,2,0:T(8,128)(2,1)}, bf16[4,128,3072]{2,1,0:T(8,128)(2,1)}, ...), condition=%wide.region_2.3_spmd, body=%wide.region_0.2_spmd.sunk | while | flops 1965359104 | bytes 109465424 | solution.py:56
  40.1 1.2 constant_dynamic-slice_fusion.4
  42.1 19.1 %add_maximum_fusion.2 = f32[128,28,28,128]{3,0,2,1:T(8,128)} fusion(f32[128]{0:T(128)S(1)} %get-tuple-element.169, bf16[128,32,32,3]{0,3,2,1:T(4,128)(2,1)S(1)} %reshape.101, bf16[5,5,3,128]{3,2,1,0:T(4,128)(2,1)S(1)} %get-tuple-element.168), kind=kOutput, calls=%fused_computation.clone.1 | convolution fusion | flops 1952448512 | bytes 52186368 | tf_op jit(solution)/shard_map/while/body/eval_jaxpr/conv_general_dilated | solution.py:33
  61.2 16.1 %reduce_sum.10 = f32[128,2,2,128]{3,0,2,1:T(8,128)S(1)} reduce(f32[128,2,14,2,14,128]{5,0,4,3,2,1:T(8,128)} %bitcast.85, f32[]{:T(128)} %constant.173.clone.1..sunk), dimensions={2,4}, to_apply=%region_1.1 | reduce | flops 12779520 | bytes 51642372 | tf_op jit(solution)/shard_map/while/body/eval_jaxpr/reduce_sum | solution.py:43
  78.2 1.2 constant_dynamic-slice_fusion.4
  80.1 19.1 %add_maximum_fusion.2 = f32[128,28,28,128]{3,0,2,1:T(8,128)} fusion(f32[128]{0:T(128)S(1)} %get-tuple-element.169, bf16[128,32,32,3]{0,3,2,1:T(4,128)(2,1)S(1)} %reshape.101, bf16[5,5,3,128]{3,2,1,0:T(4,128)(2,1)S(1)} %get-tuple-element.168), kind=kOutput, calls=%fused_computation.clone.1 | convolution fusion | flops 1952448512 | bytes 52186368 | tf_op jit(solution)/shard_map/while/body/eval_jaxpr/conv_general_dilated | solution.py:33
  99.3 16.1 %reduce_sum.10 = f32[128,2,2,128]{3,0,2,1:T(8,128)S(1)} reduce(f32[128,2,14,2,14,128]{5,0,4,3,2,1:T(8,128)} %bitcast.85, f32[]{:T(128)} %constant.173.clone.1..sunk), dimensions={2,4}, to_apply=%region_1.1 | reduce | flops 12779520 | bytes 51642372 | tf_op jit(solution)/shard_map/while/body/eval_jaxpr/reduce_sum | solution.py:43
  116.2 1.2 constant_dynamic-slice_fusion.4
  118.2 19.1 %add_maximum_fusion.2 = f32[128,28,28,128]{3,0,2,1:T(8,128)} fusion(f32[128]{0:T(128)S(1)} %get-tuple-element.169, bf16[128,32,32,3]{0,3,2,1:T(4,128)(2,1)S(1)} %reshape.101, bf16[5,5,3,128]{3,2,1,0:T(4,128)(2,1)S(1)} %get-tuple-element.168), kind=kOutput, calls=%fused_computation.clone.1 | convolution fusion | flops 1952448512 | bytes 52186368 | tf_op jit(solution)/shard_map/while/body/eval_jaxpr/conv_general_dilated | solution.py:33
  137.3 16.1 %reduce_sum.10 = f32[128,2,2,128]{3,0,2,1:T(8,128)S(1)} reduce(f32[128,2,14,2,14,128]{5,0,4,3,2,1:T(8,128)} %bitcast.85, f32[]{:T(128)} %constant.173.clone.1..sunk), dimensions={2,4}, to_apply=%region_1.1 | reduce | flops 12779520 | bytes 51642372 | tf_op jit(solution)/shard_map/while/body/eval_jaxpr/reduce_sum | solution.py:43
  154.3 1.2 constant_dynamic-slice_fusion.4
  156.3 19.1 %add_maximum_fusion.2 = f32[128,28,28,128]{3,0,2,1:T(8,128)} fusion(f32[128]{0:T(128)S(1)} %get-tuple-element.169, bf16[128,32,32,3]{0,3,2,1:T(4,128)(2,1)S(1)} %reshape.101, bf16[5,5,3,128]{3,2,1,0:T(4,128)(2,1)S(1)} %get-tuple-element.168), kind=kOutput, calls=%fused_computation.clone.1 | convolution fusion | flops 1952448512 | bytes 52186368 | tf_op jit(solution)/shard_map/while/body/eval_jaxpr/conv_general_dilated | solution.py:33
  175.4 16.1 %reduce_sum.10 = f32[128,2,2,128]{3,0,2,1:T(8,128)S(1)} reduce(f32[128,2,14,2,14,128]{5,0,4,3,2,1:T(8,128)} %bitcast.85, f32[]{:T(128)} %constant.173.clone.1..sunk), dimensions={2,4}, to_apply=%region_1.1 | reduce | flops 12779520 | bytes 51642372 | tf_op jit(solution)/shard_map/while/body/eval_jaxpr/reduce_sum | solution.py:43
  192.4 2.7 convolution_bitcast_fusion
  195.4 1.9 convert_subtract_fusion
  198.2 2.0 convolution_add_fusion
  200.3 82.0 %all-reduce.4.cloned.1.call-done = f32[512,512]{1,0:T(8,128)} async-done(((f32[512,512]{1,0:T(8,128)}), f32[512,512]{1,0:T(8,128)}) %all-reduce.4.cloned.1.call-update) | async-done | bytes 1048592 | tf_op jit(solution)/shard_map/psum | solution.py:63
  282.3 2.3 select_add_fusion
  284.6 2.6 copy.24
  287.2 1.8 fusion.19
  290.0 11.7 %cholesky.103 = f32[128,128]{1,0:T(8,128)S(1)} custom-call(f32[128,128]{1,0:T(8,128)S(1)} %cholesky.263), custom_call_target="Cholesky" | custom-call | tf_op jit(solution)/shard_map/jit(cholesky)/cholesky | solution.py:69
  302.8 9.8 %custom-call.32 = f32[1,128,128]{1,2,0:T(8,128)S(1)} custom-call(f32[1,128,128]{2,1,0:T(8,128)S(1)} %get-tuple-element.86), custom_call_target="InvertDiagBlocksLowerTriangular" | custom-call | tf_op jit(solution)/shard_map/jit(cholesky)/cholesky | solution.py:69
  312.6 2.0 constant_dynamic-update-slice_fusion.4
  314.6 1.3 convolution_subtract_fusion.4
  315.9 12.1 %cholesky.215 = f32[128,128]{1,0:T(8,128)S(1)} custom-call(f32[128,128]{1,0:T(8,128)S(1)} %cholesky.267), custom_call_target="Cholesky" | custom-call | tf_op jit(solution)/shard_map/jit(cholesky)/cholesky | solution.py:69
  328.6 9.8 %custom-call.33 = f32[1,128,128]{1,2,0:T(8,128)S(1)} custom-call(f32[1,128,128]{2,1,0:T(8,128)S(1)} %get-tuple-element.83), custom_call_target="InvertDiagBlocksLowerTriangular" | custom-call | tf_op jit(solution)/shard_map/jit(cholesky)/cholesky | solution.py:69
  339.4 1.4 convolution_subtract_fusion.5
  340.8 11.7 %cholesky.236 = f32[128,128]{1,0:T(8,128)S(1)} custom-call(f32[128,128]{1,0:T(8,128)S(1)} %cholesky.272), custom_call_target="Cholesky" | custom-call | tf_op jit(solution)/shard_map/jit(cholesky)/cholesky | solution.py:69
  353.1 9.8 %custom-call.34 = f32[1,128,128]{1,2,0:T(8,128)S(1)} custom-call(f32[1,128,128]{2,1,0:T(8,128)S(1)} %get-tuple-element.80), custom_call_target="InvertDiagBlocksLowerTriangular" | custom-call | tf_op jit(solution)/shard_map/jit(cholesky)/cholesky | solution.py:69
  363.8 1.4 convolution_subtract_fusion.6
  365.2 11.9 %cholesky.253 = f32[128,128]{1,0:T(8,128)S(1)} custom-call(f32[128,128]{1,0:T(8,128)S(1)} %convolution_subtract_fusion.6), custom_call_target="Cholesky" | custom-call | tf_op jit(solution)/shard_map/jit(cholesky)/cholesky | solution.py:69
  382.1 2.3 select_select_fusion
  384.4 14.6 %while.12 = (s32[]{:T(128)}, f32[512,512]{1,0:T(8,128)}, s32[4,2]{0,1:T(2,128)S(1)}, f32[4,128,128]{2,1,0:T(8,128)}, s32[]{:T(128)}) while((s32[]{:T(128)}, f32[512,512]{1,0:T(8,128)}, s32[4,2]{0,1:T(2,128)S(1)}, f32[4,128,128]{2,1,0:T(8,128)}, s32[]{:T(128)}) %tuple.52), condition=%wide.while_cond, body=%wide.while_body.sunk | while | flops 2 | bytes 132705 | solution.py:14
  385.1 3.0 bitcast_dynamic-update-slice_fusion.2
  388.7 3.0 bitcast_dynamic-update-slice_fusion.2
  392.4 3.0 bitcast_dynamic-update-slice_fusion.2
  396.1 2.9 bitcast_dynamic-update-slice_fusion.2
  399.0 40.1 %custom-call.35 = f32[4,128,128]{1,2,0:T(8,128)S(1)} custom-call(f32[4,128,128]{2,1,0:T(8,128)} %get-tuple-element.41), custom_call_target="InvertDiagBlocksLowerTriangular" | custom-call | tf_op jit(solution)/shard_map/triangular_solve | solution.py:14
  439.1 28.5 %all-reduce.6.cloned.1.call-done = f32[512,1000]{0,1:T(8,128)} async-done(((f32[512,1000]{0,1:T(8,128)}), f32[512,1000]{0,1:T(8,128)}) %all-reduce.6.cloned.1.call-update) | async-done | bytes 2048016 | tf_op jit(solution)/shard_map/psum | solution.py:66
  467.6 1.9 broadcast_multiply_fusion
  474.4 1.8 fusion.16
  481.0 1.2 fusion.52
  482.2 1.8 fusion.13
  486.4 1.7 add_convert_fusion
  488.2 31.7 %reduce-scatter.2.cloned.1.call-done = bf16[64,1000]{1,0:T(8,128)(2,1)} async-done(((bf16[512,1000]{1,0:T(8,128)(2,1)}), bf16[64,1000]{1,0:T(8,128)(2,1)}) %reduce-scatter.2.cloned.1.call-update) | async-done | bytes 128016 | tf_op jit(solution)/shard_map/reduce_scatter | solution.py:72
  519.8 1.6 convert_subtract_fusion.1
  (83 shorter events, 32.2 us)
Async XLA Ops:
  7.2 32.9 %all-gather.2.cloned.1.call-start = ((), (), s32[]{:S(2)}) async-start(), calls=%async_computation.1 | async-start | bytes 3538944 | tf_op jit(solution)/shard_map/all_gather | solution.py:52
  7.9 274.4 %all-reduce.4.cloned.1.call-start = ((), (), s32[]{:S(2)}) async-start(), calls=%async_computation.2 | async-start | bytes 2097152 | tf_op jit(solution)/shard_map/psum | solution.py:63
  8.7 31.4 %copy-start.5 = (f32[128]{0:T(128)S(1)}, f32[128]{0:T(128)}, u32[]{:S(2)}) copy-start(f32[128]{0:T(128)} %param.11) | copy-start | bytes 1540
  192.4 3.0 copy-start.4
  195.1 2.1 copy-start.1
  195.1 272.5 %all-reduce.6.cloned.1.call-start = ((), (), s32[]{:S(2)}) async-start(), calls=%async_computation.3 | async-start | bytes 4096000 | tf_op jit(solution)/shard_map/psum | solution.py:66
  289.0 1.0 copy-start.3
  377.1 7.3 %copy-start.6 = (s32[4]{0:T(128)S(1)}, s32[4]{0:T(128)}, u32[]{:S(2)}) copy-start(s32[4]{0:T(128)} %iota_multiply_fusion) | copy-start | bytes 52
  377.1 142.7 %reduce-scatter.2.cloned.1.call-start = ((), (), s32[]{:S(2)}) async-start(), calls=%async_computation.4 | async-start | bytes 1179648 | tf_op jit(solution)/shard_map/reduce_scatter | solution.py:72
  467.6 2.8 copy-start.2
  485.1 1.3 copy-start
Sparse Core Ops, SparseCore 0:
  9.7 30.3 all-gather.1
  195.2 86.9 all-reduce.3
  377.2 90.3 all-reduce.5
  488.3 31.4 reduce-scatter.1
where the time goes:
time: 533 us; the launch traced here: 528 us
  other arithmetic  198 us (37%)
  waiting for transfers between devices  171 us (32%)
  matrix products  108 us (20%)
  local copies, waits for them, and re-layouts  34.7 us (7%)
  between operations  16.6 us (3%)
    psum x1, waiting for transfers between devices, shards(): gram = lax.psum(left_product(feats, feats), 'dp')  82 us
    another operation x14, other arithmetic, shards(): factor = jnp.linalg.cholesky(gram)  80.7 us
    conv_general_dilated x4, matrix products, conv_pool(): lax.conv_general_dilated(pics, kernel, (1, 1), 'VALID', dimension_numbers...  76.5 us
    reduce_sum x4, other arithmetic, conv_pool(): response.reshape(count, 2, half, 2, half, filt_count).mean(axis=(2, 4))  64.5 us
    another operation x4, other arithmetic, chol_solve(): lax.linalg.triangular_solve(factor, middle, left_side=True, lower=True, t...  43.1 us
    reduce_scatter x1, waiting for transfers between devices, shards(): lax.psum_scatter((jnp.dot(feats, sol_upper, preferred_element_type=jnp.fl...  31.7 us
    psum x1, waiting for transfers between devices, shards(): cross = lax.psum(cross, 'dp')  28.5 us
    all_gather x1, waiting for transfers between devices, shards(): piece = lax.all_gather(images, 'feat', axis=0, tiled=True)  28 us
  transfers between devices with their start and end apart: 4, of which 4 were waited for; matrix products, arithmetic and copies ran while one was open for 13% of the time, Pallas kernels for 0%

commit v1 on v0

--- a/solution.py
+++ b/solution.py
@@ -63,7 +63,7 @@
     gram = lax.psum(left_product(feats, feats), "dp")
     cross = left_product(feats, res_upper) + left_product(feats, res_lower)
     cross, gram = lax.optimization_barrier((cross, gram))
-    cross = lax.psum(cross, "dp")
+    cross = jnp.sum(lax.all_gather(cross, "dp"), axis=0)
     gram = gram / total_images + 0.5 * jnp.eye(width, dtype=jnp.float32)
     cross = cross / total_images
     factor = jnp.linalg.cholesky(gram)

time: 533 us -> 566 us (1.062)
  local copies, waits for them, and re-layouts: 34.7 us -> 49.1 us
  waiting for transfers between devices: 171 us -> 185 us
    all_gather x0 -> x1, waiting for transfers between devices: none -> 41.2 us  [shards(): cross = jnp.sum(lax.all_gather(cross, 'dp'), axis=0)]
    psum x1 -> x0, waiting for transfers between devices: 28.5 us -> none  [shards(): cross = lax.psum(cross, 'dp')]
    unnamed x15 -> x14, local copies, waits for them, and re-layouts: 4.41 us -> 21.5 us
    reduce_sum x0 -> x1, other arithmetic: none -> 6.02 us  [shards(): cross = jnp.sum(lax.all_gather(cross, 'dp'), axis=0)]
  transfers between devices with their start and end apart: 4 -> 4, of which waited for: 4 -> 4; matrix products, arithmetic and copies ran while one was open for 13% -> 28% of each run, Pallas kernels for 0% -> 0%
where the time goes in v1:
time: 566 us; the launch traced here: 560 us
  other arithmetic  201 us (36%)
  waiting for transfers between devices  185 us (33%)
  matrix products  108 us (19%)
  local copies, waits for them, and re-layouts  49.1 us (9%)
  between operations  16.6 us (3%)
    psum x1, waiting for transfers between devices, shards(): gram = lax.psum(left_product(feats, feats), 'dp')  82.1 us
    another operation x14, other arithmetic, shards(): factor = jnp.linalg.cholesky(gram)  80.7 us
    conv_general_dilated x4, matrix products, conv_pool(): lax.conv_general_dilated(pics, kernel, (1, 1), 'VALID', dimension_numbers...  76.5 us
    reduce_sum x4, other arithmetic, conv_pool(): response.reshape(count, 2, half, 2, half, filt_count).mean(axis=(2, 4))  64.5 us
    another operation x4, other arithmetic, chol_solve(): lax.linalg.triangular_solve(factor, middle, left_side=True, lower=True, t...  41.8 us
    all_gather x1, waiting for transfers between devices, shards(): cross = jnp.sum(lax.all_gather(cross, 'dp'), axis=0)  41.2 us
    reduce_scatter x1, waiting for transfers between devices, shards(): lax.psum_scatter((jnp.dot(feats, sol_upper, preferred_element_type=jnp.fl...  32.3 us
    all_gather x1, waiting for transfers between devices, shards(): piece = lax.all_gather(images, 'feat', axis=0, tiled=True)  28.5 us
  transfers between devices with their start and end apart: 4, of which 4 were waited for; matrix products, arithmetic and copies ran while one was open for 28% of the time, Pallas kernels for 0%

profile of v1, /device:TPU:0, one launch (start us, length us, event | category | flops | bytes accessed | tf_op | source)
XLA Modules:
  0.0 559.9 jit_solution(5790495208748664000)
XLA Ops:
  8.7 2.9 copy.22
  11.6 28.5 %all-gather.4.cloned.1.call-done = bf16[512,3072]{1,0:T(8,128)(2,1)} async-done(((bf16[64,3072]{1,0:T(8,128)(2,1)}), bf16[512,3072]{1,0:T(8,128)(2,1)}) %all-gather.4.cloned.1.call-update) | async-done | bytes 3145744 | tf_op jit(solution)/shard_map/all_gather | solution.py:52
  40.1 152.3 %while.11 = (s32[]{:T(128)}, bf16[4,128,512]{1,2,0:T(8,128)(2,1)}, bf16[4,128,3072]{2,1,0:T(8,128)(2,1)}, bf16[5,5,3,128]{3,2,1,0:T(4,128)(2,1)S(1)}, f32[128]{0:T(128)S(1)}, /*index=5*/s32[]{:T(128)}, f32[]{:T(128)}) while((s32[]{:T(128)}, bf16[4,128,512]{1,2,0:T(8,128)(2,1)}, bf16[4,128,3072]{2,1,0:T(8,128)(2,1)}, ...), condition=%wide.region_2.3_spmd, body=%wide.region_0.2_spmd.sunk | while | flops 1965359104 | bytes 109464928 | solution.py:56
  40.1 1.2 constant_dynamic-slice_fusion.4
  42.1 19.1 %add_maximum_fusion.2 = f32[128,28,28,128]{3,0,2,1:T(8,128)} fusion(f32[128]{0:T(128)S(1)} %get-tuple-element.169, bf16[128,32,32,3]{0,3,2,1:T(4,128)(2,1)S(1)} %reshape.102, bf16[5,5,3,128]{3,2,1,0:T(4,128)(2,1)S(1)} %get-tuple-element.168), kind=kOutput, calls=%fused_computation.clone.1 | convolution fusion | flops 1952448512 | bytes 52186368 | tf_op jit(solution)/shard_map/while/body/eval_jaxpr/conv_general_dilated | solution.py:33
  61.2 16.1 %reduce_sum.21 = f32[128,2,2,128]{3,0,2,1:T(8,128)S(1)} reduce(f32[128,2,14,2,14,128]{5,0,4,3,2,1:T(8,128)} %bitcast.90, f32[]{:T(128)} %constant.174.clone.1..sunk), dimensions={2,4}, to_apply=%region_1.1 | reduce | flops 12779520 | bytes 51642372 | tf_op jit(solution)/shard_map/while/body/eval_jaxpr/reduce_sum | solution.py:43
  78.2 1.2 constant_dynamic-slice_fusion.4
  80.1 19.1 %add_maximum_fusion.2 = f32[128,28,28,128]{3,0,2,1:T(8,128)} fusion(f32[128]{0:T(128)S(1)} %get-tuple-element.169, bf16[128,32,32,3]{0,3,2,1:T(4,128)(2,1)S(1)} %reshape.102, bf16[5,5,3,128]{3,2,1,0:T(4,128)(2,1)S(1)} %get-tuple-element.168), kind=kOutput, calls=%fused_computation.clone.1 | convolution fusion | flops 1952448512 | bytes 52186368 | tf_op jit(solution)/shard_map/while/body/eval_jaxpr/conv_general_dilated | solution.py:33
  99.3 16.1 %reduce_sum.21 = f32[128,2,2,128]{3,0,2,1:T(8,128)S(1)} reduce(f32[128,2,14,2,14,128]{5,0,4,3,2,1:T(8,128)} %bitcast.90, f32[]{:T(128)} %constant.174.clone.1..sunk), dimensions={2,4}, to_apply=%region_1.1 | reduce | flops 12779520 | bytes 51642372 | tf_op jit(solution)/shard_map/while/body/eval_jaxpr/reduce_sum | solution.py:43
  116.2 1.2 constant_dynamic-slice_fusion.4
  118.2 19.1 %add_maximum_fusion.2 = f32[128,28,28,128]{3,0,2,1:T(8,128)} fusion(f32[128]{0:T(128)S(1)} %get-tuple-element.169, bf16[128,32,32,3]{0,3,2,1:T(4,128)(2,1)S(1)} %reshape.102, bf16[5,5,3,128]{3,2,1,0:T(4,128)(2,1)S(1)} %get-tuple-element.168), kind=kOutput, calls=%fused_computation.clone.1 | convolution fusion | flops 1952448512 | bytes 52186368 | tf_op jit(solution)/shard_map/while/body/eval_jaxpr/conv_general_dilated | solution.py:33
  137.3 16.1 %reduce_sum.21 = f32[128,2,2,128]{3,0,2,1:T(8,128)S(1)} reduce(f32[128,2,14,2,14,128]{5,0,4,3,2,1:T(8,128)} %bitcast.90, f32[]{:T(128)} %constant.174.clone.1..sunk), dimensions={2,4}, to_apply=%region_1.1 | reduce | flops 12779520 | bytes 51642372 | tf_op jit(solution)/shard_map/while/body/eval_jaxpr/reduce_sum | solution.py:43
  156.3 19.1 %add_maximum_fusion.2 = f32[128,28,28,128]{3,0,2,1:T(8,128)} fusion(f32[128]{0:T(128)S(1)} %get-tuple-element.169, bf16[128,32,32,3]{0,3,2,1:T(4,128)(2,1)S(1)} %reshape.102, bf16[5,5,3,128]{3,2,1,0:T(4,128)(2,1)S(1)} %get-tuple-element.168), kind=kOutput, calls=%fused_computation.clone.1 | convolution fusion | flops 1952448512 | bytes 52186368 | tf_op jit(solution)/shard_map/while/body/eval_jaxpr/conv_general_dilated | solution.py:33
  175.4 16.1 %reduce_sum.21 = f32[128,2,2,128]{3,0,2,1:T(8,128)S(1)} reduce(f32[128,2,14,2,14,128]{5,0,4,3,2,1:T(8,128)} %bitcast.90, f32[]{:T(128)} %constant.174.clone.1..sunk), dimensions={2,4}, to_apply=%region_1.1 | reduce | flops 12779520 | bytes 51642372 | tf_op jit(solution)/shard_map/while/body/eval_jaxpr/reduce_sum | solution.py:43
  192.4 2.7 convolution_bitcast_fusion
  195.1 1.9 convert_subtract_fusion
  198.0 2.0 convolution_add_fusion
  200.1 82.1 %all-reduce.3.cloned.1.call-done = f32[512,512]{1,0:T(8,128)} async-done(((f32[512,512]{1,0:T(8,128)}), f32[512,512]{1,0:T(8,128)}) %all-reduce.3.cloned.1.call-update) | async-done | bytes 1048592 | tf_op jit(solution)/shard_map/psum | solution.py:63
  282.5 2.3 select_add_fusion
  284.8 2.6 copy.24
  287.4 1.8 fusion.19
  290.1 11.7 %cholesky.103 = f32[128,128]{1,0:T(8,128)S(1)} custom-call(f32[128,128]{1,0:T(8,128)S(1)} %cholesky.263), custom_call_target="Cholesky" | custom-call | tf_op jit(solution)/shard_map/jit(cholesky)/cholesky | solution.py:69
  303.0 9.8 %custom-call.32 = f32[1,128,128]{1,2,0:T(8,128)S(1)} custom-call(f32[1,128,128]{2,1,0:T(8,128)S(1)} %get-tuple-element.86), custom_call_target="InvertDiagBlocksLowerTriangular" | custom-call | tf_op jit(solution)/shard_map/jit(cholesky)/cholesky | solution.py:69
  312.8 2.0 constant_dynamic-update-slice_fusion.4
  314.8 1.3 convolution_subtract_fusion.4
  316.1 11.7 %cholesky.215 = f32[128,128]{1,0:T(8,128)S(1)} custom-call(f32[128,128]{1,0:T(8,128)S(1)} %cholesky.267), custom_call_target="Cholesky" | custom-call | tf_op jit(solution)/shard_map/jit(cholesky)/cholesky | solution.py:69
  328.4 10.2 %custom-call.33 = f32[1,128,128]{1,2,0:T(8,128)S(1)} custom-call(f32[1,128,128]{2,1,0:T(8,128)S(1)} %get-tuple-element.83), custom_call_target="InvertDiagBlocksLowerTriangular" | custom-call | tf_op jit(solution)/shard_map/jit(cholesky)/cholesky | solution.py:69
  339.5 1.4 convolution_subtract_fusion.5
  341.0 11.7 %cholesky.236 = f32[128,128]{1,0:T(8,128)S(1)} custom-call(f32[128,128]{1,0:T(8,128)S(1)} %cholesky.272), custom_call_target="Cholesky" | custom-call | tf_op jit(solution)/shard_map/jit(cholesky)/cholesky | solution.py:69
  353.4 9.8 %custom-call.34 = f32[1,128,128]{1,2,0:T(8,128)S(1)} custom-call(f32[1,128,128]{2,1,0:T(8,128)S(1)} %get-tuple-element.80), custom_call_target="InvertDiagBlocksLowerTriangular" | custom-call | tf_op jit(solution)/shard_map/jit(cholesky)/cholesky | solution.py:69
  364.0 1.4 convolution_subtract_fusion.6
  365.4 11.7 %cholesky.253 = f32[128,128]{1,0:T(8,128)S(1)} custom-call(f32[128,128]{1,0:T(8,128)S(1)} %convolution_subtract_fusion.6), custom_call_target="Cholesky" | custom-call | tf_op jit(solution)/shard_map/jit(cholesky)/cholesky | solution.py:69
  382.2 2.4 select_select_fusion
  384.6 12.0 %while.12 = (s32[]{:T(128)}, f32[512,512]{1,0:T(8,128)}, s32[4,2]{0,1:T(2,128)S(1)}, f32[4,128,128]{2,1,0:T(8,128)S(1)}, s32[]{:T(128)}) while((s32[]{:T(128)}, f32[512,512]{1,0:T(8,128)}, s32[4,2]{0,1:T(2,128)S(1)}, f32[4,128,128]{2,1,0:T(8,128)S(1)}, s32[]{:T(128)}) %tuple.52), condition=%wide.while_cond, body=%wide.while_body.sunk | while | flops 2 | bytes 131189 | solution.py:14
  385.3 2.3 bitcast_dynamic-update-slice_fusion.2
  388.3 2.3 bitcast_dynamic-update-slice_fusion.2
  391.3 2.3 bitcast_dynamic-update-slice_fusion.2
  394.3 2.3 bitcast_dynamic-update-slice_fusion.2
  396.6 39.3 %custom-call.35 = f32[4,128,128]{1,2,0:T(8,128)S(1)} custom-call(f32[4,128,128]{2,1,0:T(8,128)S(1)} %get-tuple-element.41), custom_call_target="InvertDiagBlocksLowerTriangular" | custom-call | tf_op jit(solution)/shard_map/triangular_solve | solution.py:14
  435.9 41.2 %all-gather.6.cloned.1.call-done = f32[8192,1000]{0,1:T(8,128)} async-done(((f32[512,1000]{0,1:T(8,128)}), f32[8192,1000]{0,1:T(8,128)}) %all-gather.6.cloned.1.call-update) | async-done | bytes 32768016 | tf_op jit(solution)/shard_map/all_gather | solution.py:66
  477.1 17.1 %copy.27 = f32[125,8,16,512]{3,2,1,0:T(8,128)S(1)} copy(f32[125,8,16,512]{3,1,2,0:T(8,128)} %bitcast.91) | data formatting | bytes 65536000
  494.2 6.0 %bitcast_reduce_fusion = f32[512,1000]{0,1:T(8,128)S(1)} fusion(f32[125,8,16,512]{3,2,1,0:T(8,128)S(1)} %copy.27), kind=kLoop, calls=%fused_computation.7 | loop fusion | flops 7680000 | bytes 34816000 | tf_op jit(solution)/shard_map/reduce_sum | solution.py:66
  505.4 1.8 fusion.16
  512.0 1.2 fusion.52
  513.2 1.8 fusion.13
  517.4 1.7 add_convert_fusion
  519.2 32.3 %reduce-scatter.2.cloned.1.call-done = bf16[64,1000]{1,0:T(8,128)(2,1)} async-done(((bf16[512,1000]{1,0:T(8,128)(2,1)}), bf16[64,1000]{1,0:T(8,128)(2,1)}) %reduce-scatter.2.cloned.1.call-update) | async-done | bytes 128016 | tf_op jit(solution)/shard_map/reduce_scatter | solution.py:72
  551.5 1.6 convert_subtract_fusion.1
  (83 shorter events, 33.3 us)
Async XLA Ops:
  7.2 32.9 %all-gather.4.cloned.1.call-start = ((), (), s32[]{:S(2)}) async-start(), calls=%async_computation.1 | async-start | bytes 3538944 | tf_op jit(solution)/shard_map/all_gather | solution.py:52
  7.9 274.3 %all-reduce.3.cloned.1.call-start = ((), (), s32[]{:S(2)}) async-start(), calls=%async_computation.2 | async-start | bytes 2097152 | tf_op jit(solution)/shard_map/psum | solution.py:63
  8.7 31.4 %copy-start.5 = (f32[128]{0:T(128)S(1)}, f32[128]{0:T(128)}, u32[]{:S(2)}) copy-start(f32[128]{0:T(128)} %param.11) | copy-start | bytes 1540
  192.4 2.8 copy-start.4
  195.1 2.0 copy-start.1
  195.1 282.0 %all-gather.6.cloned.1.call-start = ((), (), s32[]{:S(2)}) async-start(), calls=%async_computation.4 | async-start | bytes 34816000 | tf_op jit(solution)/shard_map/all_gather | solution.py:66
  282.2 269.2 %reduce-scatter.2.cloned.1.call-start = ((), (), s32[]{:S(2)}) async-start(), calls=%async_computation.3 | async-start | bytes 1179648 | tf_op jit(solution)/shard_map/reduce_scatter | solution.py:72
  289.1 1.0 copy-start.3
  500.2 1.2 copy-start.2
  516.1 1.3 copy-start
Sparse Core Ops, SparseCore 0:
  9.7 30.3 all-gather.3
  195.2 86.9 all-reduce.2
  285.0 192.0 all-gather.5
  519.3 32.1 reduce-scatter.1
